TPU v7x, 32 devices: a whole 2x2x4 slice. The times are simulated.
32 devices in a mesh: lat: 8 (over y, x, core), lon: 4 (over z).
Axes of the slice: x: 2, y: 2, z: 4, core: 2. Of those that a mesh axis runs over, the one named last changes fastest.
Arguments:
- spec_coef: bfloat16 [1280, 2, 64, 1280], P(('lat', 'lon')), may hold values from -0.119628906 to 0.119628906
- legendre: bfloat16 [1280, 128, 1280], P(('lat', 'lon')), may hold values from -0.15625 to 0.15625
- wave_ids: int32 [1280], replicated, may hold values from 0 to 1279, each once
- dep_drow: int32 [128, 5120], P('lat', 'lon'), may hold values from -1 to 1
- dep_dlon: int32 [128, 5120], P('lat', 'lon'), may hold values from -1 to 1
- dep_frac: float32 [2, 128, 5120], P(None, 'lat', 'lon'), may hold values from 0 to 1
Outputs:
- grid: bfloat16 [64, 128, 5120], P(None, 'lat', 'lon')
- departed: bfloat16 [64, 128, 5120], P(None, 'lat', 'lon')
Inputs may be any that keep to these rules, and one draw needn't show every extreme that they name: `wave_ids`: each zonal wavenumber 0 to 1279 stands in exactly one storage row.
All inputs are finite; a program needn't handle non-finite values.
Results may differ from a plain program's by a relative error of at most 0.0059.
Values may be sent and summed in bfloat16 or wider, within the bound.
No kernel may reach another device: no remote copies, remote signals or barrier semaphores. Data moves between devices by JAX's collectives and lax.ppermute only.
A program may use at most 128 MiB of HBM per device.

v0:
```python
import math
import jax
import jax.numpy as jnp
from jax import lax
from jax.sharding import PartitionSpec as P

REACH = 1


def padded_2(cells, sides, width, closed):
    for axis, dim in sides:
        count = lax.axis_size(axis)
        ends = count if closed else count - 1
        head = lax.slice_in_dim(cells, 0, width, axis=dim)
        tail = lax.slice_in_dim(cells, cells.shape[dim] - width, cells.shape[dim], axis=dim)
        cells = jnp.concatenate(
            [
                lax.ppermute(tail, axis, [(i, (i + 1) % count) for i in range(ends)]),
                cells,
                lax.ppermute(head, axis, [((i + 1) % count, i) for i in range(ends)]),
            ],
            axis=dim,
        )
    return cells


def wave_table(wave_order, lon_start, lon_count, cycle_size):
    longitude = lon_start + jnp.arange(lon_count, dtype=jnp.int32)
    phase_index = wave_order[:, None] * longitude[None, :] % cycle_size
    theta = phase_index.astype(jnp.float32) * (2.0 * math.pi / cycle_size)
    factor = jnp.where(wave_order == 0, 1.0, 2.0).astype(jnp.float32)[:, None]
    return jnp.stack([factor * jnp.cos(theta), -factor * jnp.sin(theta)]).astype(jnp.bfloat16)


def shift_weight(offsets, frac, shift):
    zeros = jnp.zeros_like(frac)
    lower = jnp.where(offsets == shift, 1.0 - frac, zeros)
    higher = jnp.where(offsets == shift - 1, frac, zeros)
    return lower + higher


def per_device(spec_coef, legendre, wave_ids, dep_drow, dep_dlon, dep_frac):
    lat_count = lax.axis_size("lat")
    lon_parts = lax.axis_size("lon")
    local_waves = spec_coef.shape[0]
    level_fields = spec_coef.shape[2]
    degree_count = spec_coef.shape[3]
    all_waves = wave_ids.shape[0]
    row_count = dep_drow.shape[0]
    sector_width = dep_drow.shape[1]
    cycle_size = sector_width * lon_parts
    quarter = level_fields // lon_parts
    device = lax.axis_index("lat") * lon_parts + lax.axis_index("lon")
    local_ids = lax.dynamic_slice_in_dim(wave_ids, device * local_waves, local_waves)
    keep = jnp.arange(degree_count, dtype=jnp.int32)[None, :] >= local_ids[:, None]
    kept = jnp.where(keep[:, None, None, :], spec_coef, jnp.zeros((), spec_coef.dtype))
    kept = kept.reshape(local_waves, 2, lon_parts, quarter, degree_count)
    matrices = legendre.reshape(local_waves, lat_count, row_count, degree_count)
    fourier = jnp.einsum(
        "mrbqn,mapn->mabprq", kept, matrices, preferred_element_type=jnp.float32
    ).astype(jnp.bfloat16)
    moved = lax.all_to_all(
        lax.all_to_all(fourier, "lat", split_axis=1, concat_axis=0, tiled=True),
        "lon",
        split_axis=2,
        concat_axis=0,
        tiled=True,
    )
    wave_order = (
        wave_ids.reshape(lat_count, lon_parts, local_waves).transpose(1, 0, 2).reshape(all_waves)
    )
    moved = moved.reshape(all_waves, row_count, 2, quarter)
    table = wave_table(wave_order, lax.axis_index("lon") * sector_width, sector_width, cycle_size)
    grid = jnp.einsum(
        "mprq,rmx->qpx",
        lax.all_gather(moved, "lon", axis=3, tiled=True),
        table,
        preferred_element_type=jnp.float32,
    ).astype(jnp.bfloat16)
    margin = REACH + 1
    tall = padded_2(grid, (("lat", 1),), margin, False)
    padded = padded_2(tall, (("lon", 2),), margin, True)
    frac_row = dep_frac[0]
    frac_col = dep_frac[1]
    col_weights = [shift_weight(dep_dlon, frac_col, shift) for shift in range(-REACH, REACH + 2)]
    total = jnp.zeros((level_fields, row_count, sector_width), jnp.float32)
    for row_shift in range(-REACH, REACH + 2):
        band = padded[:, margin + row_shift : margin + row_shift + row_count, :]
        along = jnp.zeros((level_fields, row_count, sector_width), jnp.float32)
        for place, col_shift in enumerate(range(-REACH, REACH + 2)):
            window = band[:, :, margin + col_shift : margin + col_shift + sector_width].astype(
                jnp.float32
            )
            along = along + col_weights[place][None] * window
        total = total + shift_weight(dep_drow, frac_row, row_shift)[None] * along
    return (grid, total.astype(jnp.bfloat16))


def solution(mesh):
    in_specs = (
        P(("lat", "lon"), None, None, None),
        P(("lat", "lon"), None, None),
        P(),
        P("lat", "lon"),
        P("lat", "lon"),
        P(None, "lat", "lon"),
    )
    out_specs = (P(None, "lat", "lon"), P(None, "lat", "lon"))
    return jax.shard_map(
        per_device, mesh=mesh, in_specs=in_specs, out_specs=out_specs, check_vma=False
    )
```

profile of v0, /device:TPU:5, one launch (start us, length us, event | category | flops | bytes accessed | tf_op | source)
XLA Modules:
  0.0 315.4 jit_solution(18104308854111554694)
XLA Ops:
  7.2 0.0 all-gather.2.cloned.1.call-start
  7.2 0.8 dynamic_slice.3
  8.0 0.1 iota_compare_fusion
  8.1 7.0 %broadcast_select_fusion = bf16[40,2,64,1280]{3,2,1,0:T(8,128)(2,1)S(1)} fusion(bf16[40,2,64,1280]{3,2,1,0:T(8,128)(2,1)} %param.6, pred[40,1280]{1,0:T(8,128)(4,1)S(1)} %iota_compare_fusion), kind=kLoop, calls=%fused_computation | loop fusion | flops 6553600 | bytes 26265600 | tf_op jit(solution)/shard_map/jit(_where)/select_n | solution.py:56
  15.1 19.7 %convert_bitcast_fusion = bf16[40,8,4,16,2,16]{3,5,1,2,4,0:T(8,128)(2,1)} fusion(bf16[40,2,4,16,1280,1]{4,3,5,2,1,0:T(8,128)(2,1)S(1)} %bitcast.93, bf16[40,8,16,1280,1,1]{3,2,1,5,4,0:T(8,128)(2,1)} %bitcast.97), kind=kOutput, calls=%fused_computation.1 | convolution fusion | flops 1678376960 | bytes 27525120 | tf_op jit(solution)/shard_map/mrbqn,mapn->mabprq/dot_general | solution.py:59
  34.9 17.7 %copy.20 = bf16[40,8,4,16,2,16]{0,5,4,3,2,1:T(8,128)(2,1)} copy(bf16[40,8,4,16,2,16]{3,5,1,2,4,0:T(8,128)(2,1)} %convert_bitcast_fusion) | data formatting | bytes 2621440 | tf_op jit(solution)/shard_map/convert_element_type | solution.py:61
  52.6 8.1 %reshape.245 = bf16[8,2,40960]{2,1,0:T(2,128)(2,1)S(1)} reshape(bf16[8,4,16,2,16,40]{5,4,3,2,1,0:T(8,128)(2,1)} %bitcast.92) | data formatting | bytes 2621440
  60.7 20.0 %all_to_all.33 = bf16[8,2,40960]{2,1,0:T(2,128)(2,1)S(1)} all-to-all(bf16[8,2,40960]{2,1,0:T(2,128)(2,1)S(1)} %reshape.245), channel_id=1, replica_groups=mesh['lat'=8,'lon'=4] {'lat'}, dimensions={0} | all-to-all | bytes 2621440 | tf_op jit(solution)/shard_map/all_to_all | solution.py:63
  80.7 7.2 %reshape.246 = bf16[8,4,16,2,16,40]{5,4,3,2,1,0:T(8,128)(2,1)} reshape(bf16[8,2,40960]{2,1,0:T(2,128)(2,1)S(1)} %all_to_all.33) | data formatting | bytes 2621440
  87.9 3.0 bitcast_bitcast_fusion
  90.9 6.8 %copy.21 = bf16[8,40,1,4,16,2,16]{1,0,6,5,4,3,2:T(8,128)(2,1)} copy(bf16[8,40,1,4,16,2,16]{1,6,5,4,3,0,2:T(8,128)(2,1)S(1)} %bitcast_bitcast_fusion) | data formatting | bytes 2621440 | tf_op jit(solution)/shard_map/all_to_all | solution.py:63
  97.7 5.5 %all_to_all.27 = bf16[320,1,4,16,2,16]{0,5,4,3,2,1:T(8,128)(2,1)S(1)} reshape(bf16[8,40,1,4,16,2,16]{1,0,6,5,4,3,2:T(8,128)(2,1)} %copy.21) | data formatting | bytes 2621440 | tf_op jit(solution)/shard_map/all_to_all | solution.py:63
  103.2 0.0 copy-start.3
  103.2 40.5 %all_to_all.34 = bf16[320,1,4,16,2,16]{0,5,4,3,1,2:T(8,128)(2,1)S(1)} all-to-all(bf16[320,1,4,16,2,16]{0,5,4,3,1,2:T(8,128)(2,1)S(1)} %bitcast.95), channel_id=1, replica_groups=mesh['lat'=8,'lon'=4] {'lon'}, dimensions={2} | all-to-all | bytes 2621440 | tf_op jit(solution)/shard_map/all_to_all | solution.py:62
  143.8 1.2 copy.23
  145.0 2.1 reshape.240
  147.0 0.0 all-gather.2.cloned.1.call-update
  147.1 0.0 copy-done.3
  147.1 0.1 reshape.236
  147.2 0.1 reshape.237
  147.3 29.5 %multiply_convert_fusion.1 = (bf16[1,1280,1280]{2,1,0:T(8,128)(2,1)S(1)}, bf16[1,1280,1280]{2,1,0:T(8,128)(2,1)}) fusion(s32[1280]{0:T(1024)S(1)} %iota_add_fusion, s32[1280]{0:T(1024)S(1)} %reshape.237, f32[1280]{0:T(1024)S(1)} %get-tuple-element.30, f32[1280]{0:T(1024)S(1)} %get-tuple-element.31), kind=kLoop, calls=%fused_computation.10 | loop fusion | flops 21299200 | bytes 6574080 | tf_op jit(solution)/shard_map/convert
  176.8 68.7 %all-gather.2.cloned.1.call-done = bf16[1280,16,2,64]{0,3,2,1:T(8,128)(2,1)} async-done(((bf16[1280,16,2,16]{0,3,2,1:T(8,128)(2,1)}), bf16[1280,16,2,64]{0,3,2,1:T(8,128)(2,1)}) %all-gather.2.cloned.1.call-update) | async-done | bytes 5242896 | tf_op jit(solution)/shard_map/all_gather | solution.py:76
  245.6 9.9 %fusion.8 = bf16[64,16,1280]{2,0,1:T(8,128)(2,1)S(1)} fusion(bf16[1280,16,2,64]{0,3,2,1:T(8,128)(2,1)} %all-gather.2.cloned.1.call-done, bf16[1,1280,1280]{2,1,0:T(8,128)(2,1)} %get-tuple-element.29, bf16[1,1280,1280]{2,1,0:T(8,128)(2,1)S(1)} %get-tuple-element.28), kind=kOutput, calls=%fused_computation.19 | convolution fusion | flops 6725304320 | bytes 14417920 | tf_op jit(solution)/shard_map/mprq,rmx->qpx/dot_general | solution.py:74
  255.5 0.0 copy-start
  255.5 0.0 copy-start.1
  255.5 0.0 copy-start.2
  255.6 3.6 %collective-permute-start = (bf16[64,2,1280]{2,0,1:T(8,128)(2,1)S(1)}, bf16[64,2,1280]{2,0,1:T(8,128)(2,1)S(1)}, u32[]{:S(2)}, u32[]{:S(2)}) collective-permute-start(bf16[64,2,1280]{2,0,1:T(8,128)(2,1)S(1)} %get-tuple-element.14), channel_id=1, source_target_pairs={{0,4},{4,8},{8,12},{12,16},{16,20},{20,24},{24,28},{1,5},{5,9},{9,... | collective-permute-start | bytes 983048 | tf_op jit(solution)/shard_map/ppermute | solution.py:18
  259.2 1.9 collective-permute-start.1
  261.1 2.1 collective-permute-done
  263.2 4.4 %collective-permute-done.1 = bf16[64,2,1280]{2,0,1:T(8,128)(2,1)S(1)} collective-permute-done((bf16[64,2,1280]{2,0,1:T(8,128)(2,1)S(1)}, bf16[64,2,1280]{2,0,1:T(8,128)(2,1)S(1)}, u32[]{:S(2)}, u32[]{:S(2)}) %collective-permute-start.1) | collective-permute-done | bytes 327712 | tf_op jit(solution)/shard_map/ppermute | solution.py:20
  267.6 0.2 pad_maximum_fusion.5
  267.8 0.1 collective-permute-start.2
  267.8 3.3 %collective-permute-start.3 = (bf16[64,20,2]{2,0,1:T(8,128)(2,1)S(1)}, bf16[64,20,2]{2,0,1:T(8,128)(2,1)S(1)}, u32[]{:S(2)}, u32[]{:S(2)}) collective-permute-start(bf16[64,20,2]{2,0,1:T(8,128)(2,1)S(1)} %get-tuple-element.13), channel_id=1, source_target_pairs={{1,0},{2,1},{3,2},{0,3},{5,4},{6,5},{7,6},{4,7},{9,8},{10,9},{11,1... | collective-permute-start | bytes 15368 | tf_op jit(solution)/shard_map/ppermute | solution.py:20
  271.1 0.0 copy-done
  271.1 0.0 copy-done.1
  271.1 0.0 copy-done.2
  271.1 0.1 fusion.14
  271.2 2.9 copy.24
  274.1 5.1 %collective-permute-done.2 = bf16[64,20,2]{2,0,1:T(8,128)(2,1)S(1)} collective-permute-done((bf16[64,20,2]{2,0,1:T(8,128)(2,1)S(1)}, bf16[64,20,2]{2,0,1:T(8,128)(2,1)S(1)}, u32[]{:S(2)}, u32[]{:S(2)}) %collective-permute-start.2) | collective-permute-done | bytes 5152 | tf_op jit(solution)/shard_map/ppermute | solution.py:18
  279.3 5.5 %collective-permute-done.3 = bf16[64,20,2]{2,0,1:T(8,128)(2,1)S(1)} collective-permute-done((bf16[64,20,2]{2,0,1:T(8,128)(2,1)S(1)}, bf16[64,20,2]{2,0,1:T(8,128)(2,1)S(1)}, u32[]{:S(2)}, u32[]{:S(2)}) %collective-permute-start.3) | collective-permute-done | bytes 5152 | tf_op jit(solution)/shard_map/ppermute | solution.py:20
  284.8 2.7 maximum_maximum_fusion
  287.5 18.1 %add_convert_fusion = bf16[64,16,1280]{2,0,1:T(8,128)(2,1)S(1)} fusion(bf16[64,16,1280]{2,0,1:T(8,128)(2,1)S(1)} %fusion.8, bf16[64,2,1280]{2,0,1:T(8,128)(2,1)S(1)} %collective-permute-done.1, bf16[64,20,1282]{2,0,1:T(8,128)(2,1)S(1)} %get-tuple-element.11, bf16[64,20,1282]{2,0,1:T(8,128)(2,1)S(1)} %get-tuple-element.10, ...), kind=kLoop, calls=%fused_computation.16 | loop fusion | flops 72089600 | bytes 38010880 | tf_op jit(solution)/shard_map/convert_element_type | solution.py:96
  305.6 2.9 copy.25
  (4 shorter events, 0.1 us)
Async XLA Ops:
  7.2 238.4 %all-gather.2.cloned.1.call-start = ((), (), s32[]{:S(2)}) async-start(), calls=%async_computation.2 | async-start | bytes 6553600 | tf_op jit(solution)/shard_map/all_gather | solution.py:76
  103.2 43.8 %copy-start.3 = (s32[1280]{0:T(1024)S(1)}, s32[1280]{0:T(1024)}, u32[]{:S(2)}) copy-start(s32[1280]{0:T(1024)} %param.8) | copy-start | bytes 15364
  255.5 15.6 %copy-start = (f32[2,16,1280]{2,1,0:T(8,128)S(1)}, f32[2,16,1280]{2,1,0:T(8,128)}, u32[]{:S(2)}) copy-start(f32[2,16,1280]{2,1,0:T(8,128)} %param.11) | copy-start | bytes 491524
  255.5 15.6 %copy-start.1 = (s32[16,1280]{1,0:T(8,128)S(1)}, s32[16,1280]{1,0:T(8,128)}, u32[]{:S(2)}) copy-start(s32[16,1280]{1,0:T(8,128)} %param.9) | copy-start | bytes 245764
  255.5 15.6 %copy-start.2 = (s32[16,1280]{1,0:T(8,128)S(1)}, s32[16,1280]{1,0:T(8,128)}, u32[]{:S(2)}) copy-start(s32[16,1280]{1,0:T(8,128)} %param.10) | copy-start | bytes 245764
  255.6 7.6 %collective-permute-start = (bf16[64,2,1280]{2,0,1:T(8,128)(2,1)S(1)}, bf16[64,2,1280]{2,0,1:T(8,128)(2,1)S(1)}, u32[]{:S(2)}, u32[]{:S(2)}) collective-permute-start(bf16[64,2,1280]{2,0,1:T(8,128)(2,1)S(1)} %get-tuple-element.14), channel_id=1, source_target_pairs={{0,4},{4,8},{8,12},{12,16},{16,20},{20,24},{24,28},{1,5},{5,9},{9,... | collective-permute-start | bytes 983048 | tf_op jit(solution)/shard_map/ppermute | solution.py:18
  259.2 8.4 %collective-permute-start.1 = (bf16[64,2,1280]{2,0,1:T(8,128)(2,1)S(1)}, bf16[64,2,1280]{2,0,1:T(8,128)(2,1)S(1)}, u32[]{:S(2)}, u32[]{:S(2)}) collective-permute-start(bf16[64,2,1280]{2,0,1:T(8,128)(2,1)S(1)} %get-tuple-element.15), channel_id=1, source_target_pairs={{4,0},{8,4},{12,8},{16,12},{20,16},{24,20},{28,24},{5,1},{9,5},{13... | collective-permute-start | bytes 983048 | tf_op jit(solution)/shard_map/ppermute | solution.py:20
  267.8 11.5 %collective-permute-start.2 = (bf16[64,20,2]{2,0,1:T(8,128)(2,1)S(1)}, bf16[64,20,2]{2,0,1:T(8,128)(2,1)S(1)}, u32[]{:S(2)}, u32[]{:S(2)}) collective-permute-start(bf16[64,20,2]{2,0,1:T(8,128)(2,1)S(1)} %get-tuple-element.12), channel_id=1, source_target_pairs={{0,1},{1,2},{2,3},{3,0},{4,5},{5,6},{6,7},{7,4},{8,9},{9,10},{10,1... | collective-permute-start | bytes 15368 | tf_op jit(solution)/shard_map/ppermute | solution.py:18
  267.8 16.9 %collective-permute-start.3 = (bf16[64,20,2]{2,0,1:T(8,128)(2,1)S(1)}, bf16[64,20,2]{2,0,1:T(8,128)(2,1)S(1)}, u32[]{:S(2)}, u32[]{:S(2)}) collective-permute-start(bf16[64,20,2]{2,0,1:T(8,128)(2,1)S(1)} %get-tuple-element.13), channel_id=1, source_target_pairs={{1,0},{2,1},{3,2},{0,3},{5,4},{6,5},{7,6},{4,7},{9,8},{10,9},{11,1... | collective-permute-start | bytes 15368 | tf_op jit(solution)/shard_map/ppermute | solution.py:20
Sparse Core Ops, SparseCore 0:
  147.2 98.3 all-gather.1
where the time goes:
time: 316 us; the launch traced here: 315 us
  waiting for transfers between devices  85.9 us (27%)
  blocking collectives  60.6 us (19%)
  local copies, waits for them, and re-layouts  58.5 us (19%)
  other arithmetic  57.8 us (18%)
  matrix products  29.6 us (9%)
  between operations  14.2 us (4%)
  starting transfers between devices  8.87 us (3%)
    all_gather x1, waiting for transfers between devices, per_device(): lax.all_gather(moved, 'lon', axis=3, tiled=True)  68.7 us
    all_to_all x1, blocking collectives, per_device(): lax.all_to_all(lax.all_to_all(fourier, 'lat', split_axis=1, concat_axis=0...  40.5 us
    another operation x1, other arithmetic  29.5 us
    unnamed x12, local copies, waits for them, and re-layouts  21.2 us
    all_to_all x1, blocking collectives, per_device(): lax.all_to_all(fourier, 'lat', split_axis=1, concat_axis=0, tiled=True)  20 us
    dot_general x1, matrix products, per_device(): jnp.einsum('mrbqn,mapn->mabprq', kept, matrices, preferred_element_type=j...  19.7 us
    convert_element_type x1, other arithmetic, per_device(): return (grid, total.astype(jnp.bfloat16))  18.1 us
    convert_element_type x1, local copies, waits for them, and re-layouts, per_device(): fourier = jnp.einsum('mrbqn,mapn->mabprq', kept, matrices, preferred_elem...  17.7 us
  transfers between devices with their start and end apart: 5, of which 5 were waited for; matrix products, arithmetic and copies ran while one was open for 10% of the time, Pallas kernels for 0%

commit v1 on v0

--- a/solution.py
+++ b/solution.py
@@ -5,6 +5,25 @@
 from jax.sharding import PartitionSpec as P
 
 REACH = 1
+
+
+def joined_along(tiles, dim):
+    lengths = list(tiles.shape[1:])
+    lengths[dim] *= tiles.shape[0]
+    return jnp.moveaxis(tiles, 0, dim).reshape(lengths)
+
+
+def ring_apply(x, axis, dim, work, out_dim):
+    size, index, rows = (lax.axis_size(axis), lax.axis_index(axis), x.shape[dim])
+    forward = [(i, (i + 1) % size) for i in range(size)]
+    pieces = []
+    held = x
+    for step in range(size):
+        coming = held if step == size - 1 else lax.ppermute(held, axis, forward)
+        pieces.append(work(held, (index - step) % size * rows))
+        held = coming
+    pieces = jnp.stack(pieces)[(index - jnp.arange(size)) % size]
+    return joined_along(pieces, out_dim)
 
 
 def padded_2(cells, sides, width, closed):
@@ -71,11 +90,14 @@
     )
     moved = moved.reshape(all_waves, row_count, 2, quarter)
     table = wave_table(wave_order, lax.axis_index("lon") * sector_width, sector_width, cycle_size)
-    grid = jnp.einsum(
-        "mprq,rmx->qpx",
-        lax.all_gather(moved, "lon", axis=3, tiled=True),
-        table,
-        preferred_element_type=jnp.float32,
+    grid = ring_apply(
+        moved,
+        "lon",
+        3,
+        lambda shard, at: jnp.einsum(
+            "mprq,rmx->qpx", shard, table, preferred_element_type=jnp.float32
+        ),
+        0,
     ).astype(jnp.bfloat16)
     margin = REACH + 1
     tall = padded_2(grid, (("lat", 1),), margin, False)

time: 316 us -> 306 us (0.968)
  blocking collectives: 60.6 us -> 0 us
  waiting for transfers between devices: 85.9 us -> 123 us
  starting transfers between devices: 8.87 us -> 22.9 us
  between operations: 14.2 us -> 0.86 us
  other arithmetic: 57.8 us -> 67.3 us
    ppermute x0 -> x3, waiting for transfers between devices: none -> 79.2 us  [ring_apply(): coming = held if step == size - 1 else lax.ppermute(held, axis, forward)]
    all_gather x1 -> x0, waiting for transfers between devices: 68.7 us -> none  [per_device(): lax.all_gather(moved, 'lon', axis=3, tiled=True)]
    all_to_all x2 -> x0, blocking collectives: 60.6 us -> none  [the longest x1 40.5 us: per_device(): lax.all_to_all(lax.all_to_all(fourier, 'lat', split_axis=1, concat_axis=0...]
    all_to_all x0 -> x2, waiting for transfers between devices: none -> 21 us  [the longest x1 14.3 us: per_device(): lax.all_to_all(fourier, 'lat', split_axis=1, concat_axis=0, tiled=True)]
    all_to_all x0 -> x2, starting transfers between devices: none -> 9.12 us  [the longest x1 4.58 us: per_device(): lax.all_to_all(fourier, 'lat', split_axis=1, concat_axis=0, tiled=True)]
    ppermute x2, waiting for transfers between devices: 7.2 us -> 12.4 us  [padded_2(): lax.ppermute(tail, axis, [(i, (i + 1) % count) for i in range(ends)])]
    unnamed x12 -> x16, local copies, waits for them, and re-layouts: 21.2 us -> 16.2 us
    ppermute x2, starting transfers between devices: 3.66 us -> 8.32 us  [padded_2(): lax.ppermute(tail, axis, [(i, (i + 1) % count) for i in range(ends)])]
  transfers between devices with their start and end apart: 5 -> 9, of which waited for: 5 -> 9; matrix products, arithmetic and copies ran while one was open for 10% -> 13% of each run, Pallas kernels for 0% -> 0%
where the time goes in v1:
time: 306 us; the launch traced here: 305 us
  waiting for transfers between devices  123 us (40%)
  other arithmetic  67.3 us (22%)
  local copies, waits for them, and re-layouts  58.6 us (19%)
  matrix products  32 us (10%)
  starting transfers between devices  22.9 us (7%)
    ppermute x3, waiting for transfers between devices, ring_apply(): coming = held if step == size - 1 else lax.ppermute(held, axis, forward)  79.2 us
    another operation x1, other arithmetic  29.7 us
    convert_element_type x1, other arithmetic, per_device(): return (grid, total.astype(jnp.bfloat16))  22.5 us
    dot_general x1, matrix products, per_device(): jnp.einsum('mrbqn,mapn->mabprq', kept, matrices, preferred_element_type=j...  19.7 us
    convert_element_type x1, local copies, waits for them, and re-layouts, per_device(): fourier = jnp.einsum('mrbqn,mapn->mabprq', kept, matrices, preferred_elem...  17.7 us
    unnamed x16, local copies, waits for them, and re-layouts  16.2 us
    all_to_all x3, local copies, waits for them, and re-layouts, per_device(): lax.all_to_all(fourier, 'lat', split_axis=1, concat_axis=0, tiled=True)  16.1 us
    all_to_all x1, waiting for transfers between devices, per_device(): lax.all_to_all(fourier, 'lat', split_axis=1, concat_axis=0, tiled=True)  14.3 us
  transfers between devices with their start and end apart: 9, of which 9 were waited for; matrix products, arithmetic and copies ran while one was open for 13% of the time, Pallas kernels for 0%

profile of v1, /device:TPU:5, one launch (start us, length us, event | category | flops | bytes accessed | tf_op | source)
XLA Modules:
  0.0 304.8 jit_solution(1666190829812416695)
XLA Ops:
  0.6 0.8 dynamic_slice.3
  1.4 0.1 iota_compare_fusion
  1.5 7.0 %broadcast_select_fusion = bf16[40,2,64,1280]{3,2,1,0:T(8,128)(2,1)S(1)} fusion(bf16[40,2,64,1280]{3,2,1,0:T(8,128)(2,1)} %param.6, pred[40,1280]{1,0:T(8,128)(4,1)S(1)} %iota_compare_fusion), kind=kLoop, calls=%fused_computation.1 | loop fusion | flops 6553600 | bytes 26265600 | tf_op jit(solution)/shard_map/jit(_where)/select_n | solution.py:75
  8.5 19.7 %convert_bitcast_fusion = bf16[40,8,4,16,2,16]{3,5,1,2,4,0:T(8,128)(2,1)} fusion(bf16[40,2,4,16,1280,1]{4,3,5,2,1,0:T(8,128)(2,1)S(1)} %bitcast.127, bf16[40,8,16,1280,1,1]{3,2,1,5,4,0:T(8,128)(2,1)} %bitcast.130), kind=kOutput, calls=%fused_computation.2 | convolution fusion | flops 1678376960 | bytes 27525120 | tf_op jit(solution)/shard_map/mrbqn,mapn->mabprq/dot_general | solution.py:78
  28.3 17.7 %copy.16 = bf16[40,8,4,16,2,16]{0,5,4,3,2,1:T(8,128)(2,1)} copy(bf16[40,8,4,16,2,16]{3,5,1,2,4,0:T(8,128)(2,1)} %convert_bitcast_fusion) | data formatting | bytes 2621440 | tf_op jit(solution)/shard_map/convert_element_type | solution.py:80
  45.9 0.0 copy-start.6
  45.9 9.0 %reshape.307 = bf16[8,2,40960]{2,1,0:T(2,128)(2,1)} reshape(bf16[8,4,16,2,16,40]{5,4,3,2,1,0:T(8,128)(2,1)} %bitcast.126) | data formatting | bytes 2621440
  54.9 4.6 %all-to-all-start = ((bf16[8,2,40960]{2,1,0:T(2,128)(2,1)}), bf16[8,2,40960]{2,1,0:T(2,128)(2,1)S(1)}, u32[]{:S(2)}, u32[]{:S(2)}) async-start(bf16[8,2,40960]{2,1,0:T(2,128)(2,1)} %reshape.307), calls=%async_computation | async-start | bytes 2621440 | tf_op jit(solution)/shard_map/all_to_all | solution.py:82
  59.5 0.0 copy-done.6
  59.5 0.1 reshape.287
  59.6 0.1 reshape.288
  59.7 14.3 %all-to-all-done = bf16[8,2,40960]{2,1,0:T(2,128)(2,1)S(1)} async-done(((bf16[8,2,40960]{2,1,0:T(2,128)(2,1)}), bf16[8,2,40960]{2,1,0:T(2,128)(2,1)S(1)}, u32[]{:S(2)}, u32[]{:S(2)}) %all-to-all-start) | async-done | bytes 1310752 | tf_op jit(solution)/shard_map/all_to_all | solution.py:82
  74.0 7.1 %reshape.308 = bf16[8,4,16,2,16,40]{5,4,3,2,1,0:T(8,128)(2,1)} reshape(bf16[8,2,40960]{2,1,0:T(2,128)(2,1)S(1)} %all-to-all-done) | data formatting | bytes 2621440
  81.1 3.0 bitcast_bitcast_fusion
  84.1 6.8 %copy.17 = bf16[8,40,1,4,16,2,16]{1,0,6,5,4,3,2:T(8,128)(2,1)} copy(bf16[8,40,1,4,16,2,16]{1,6,5,4,3,0,2:T(8,128)(2,1)S(1)} %bitcast_bitcast_fusion) | data formatting | bytes 2621440 | tf_op jit(solution)/shard_map/all_to_all | solution.py:82
  90.9 6.4 %all_to_all.27 = bf16[320,1,4,16,2,16]{0,5,4,3,2,1:T(8,128)(2,1)} reshape(bf16[8,40,1,4,16,2,16]{1,0,6,5,4,3,2:T(8,128)(2,1)} %copy.17) | data formatting | bytes 2621440 | tf_op jit(solution)/shard_map/all_to_all | solution.py:82
  97.2 4.5 %all-to-all-start.1 = ((bf16[320,1,4,16,2,16]{0,5,4,3,1,2:T(8,128)(2,1)}), bf16[320,1,4,16,2,16]{0,5,4,3,1,2:T(8,128)(2,1)S(1)}, u32[]{:S(2)}, u32[]{:S(2)}) async-start(bf16[320,1,4,16,2,16]{0,5,4,3,1,2:T(8,128)(2,1)} %bitcast.9), calls=%async_computation.1 | async-start | bytes 3145728 | tf_op jit(solution)/shard_map/all_to_all | solution.py:81
  101.8 29.7 %multiply_convert_fusion.1 = (bf16[1,1280,1280]{2,1,0:T(8,128)(2,1)}, bf16[1,1280,1280]{2,1,0:T(8,128)(2,1)}) fusion(s32[1280]{0:T(1024)S(1)} %iota_add_fusion, s32[1280]{0:T(1024)S(1)} %reshape.288, f32[1280]{0:T(1024)S(1)} %get-tuple-element.22, f32[1280]{0:T(1024)S(1)} %get-tuple-element.23), kind=kLoop, calls=%fused_computation.8 | loop fusion | flops 21299200 | bytes 6574080 | tf_op jit(solution)/shard_map/convert
  131.5 6.8 %all-to-all-done.1 = bf16[320,1,4,16,2,16]{0,5,4,3,1,2:T(8,128)(2,1)S(1)} async-done(((bf16[320,1,4,16,2,16]{0,5,4,3,1,2:T(8,128)(2,1)}), bf16[320,1,4,16,2,16]{0,5,4,3,1,2:T(8,128)(2,1)S(1)}, u32[]{:S(2)}, u32[]{:S(2)}) %all-to-all-start.1) | async-done | bytes 1310752 | tf_op jit(solution)/shard_map/all_to_all | solution.py:81
  138.2 1.2 copy.19
  139.5 1.2 reshape.291
  140.7 0.3 collective-permute-start
  141.0 0.0 copy-start.1
  141.0 0.0 copy-start.2
  141.0 4.9 %convolution_bitcast_fusion.3 = bf16[1,16,16,1280]{3,1,2,0:T(8,128)(2,1)S(1)} fusion(bf16[1280,16,2,16]{0,3,2,1:T(8,128)(2,1)S(1)} %reshape.291, bf16[1,1280,1280]{2,1,0:T(8,128)(2,1)} %get-tuple-element.21, bf16[1,1280,1280]{2,1,0:T(8,128)(2,1)} %get-tuple-element.20), kind=kOutput, calls=%fused_computation.22 | convolution fusion | flops 1690828800 | bytes 8519680 | tf_op jit(solution)/shard_map/mprq,rmx->qpx/dot_general | solution.py:97
  146.0 25.6 %collective-permute-done = bf16[1280,16,2,16]{0,3,2,1:T(8,128)(2,1)S(1)} collective-permute-done((bf16[1280,16,2,16]{0,3,2,1:T(8,128)(2,1)S(1)}, bf16[1280,16,2,16]{0,3,2,1:T(8,128)(2,1)S(1)}, u32[]{:S(2)}, u32[]{:S(2)}) %collective-permute-start) | collective-permute-done | bytes 1310752 | tf_op jit(solution)/shard_map/ppermute | solution.py:22
  171.6 0.0 collective-permute-start.1
  171.6 0.0 copy-done.1
  171.6 0.0 copy-done.2
  171.6 2.5 convolution_bitcast_fusion.2
  174.1 27.2 %collective-permute-done.1 = bf16[1280,16,2,16]{0,3,2,1:T(8,128)(2,1)S(1)} collective-permute-done((bf16[1280,16,2,16]{0,3,2,1:T(8,128)(2,1)S(1)}, bf16[1280,16,2,16]{0,3,2,1:T(8,128)(2,1)S(1)}, u32[]{:S(2)}, u32[]{:S(2)}) %collective-permute-start.1) | collective-permute-done | bytes 1310752 | tf_op jit(solution)/shard_map/ppermute | solution.py:22
  201.3 0.0 collective-permute-start.2
  201.3 2.4 convolution_bitcast_fusion.1
  203.7 26.3 %collective-permute-done.2 = bf16[1280,16,2,16]{0,3,2,1:T(8,128)(2,1)S(1)} collective-permute-done((bf16[1280,16,2,16]{0,3,2,1:T(8,128)(2,1)S(1)}, bf16[1280,16,2,16]{0,3,2,1:T(8,128)(2,1)S(1)}, u32[]{:S(2)}, u32[]{:S(2)}) %collective-permute-start.2) | collective-permute-done | bytes 1310752 | tf_op jit(solution)/shard_map/ppermute | solution.py:22
  230.0 2.4 convolution_bitcast_fusion
  232.5 0.3 pad_maximum_fusion
  232.8 2.2 gather_fusion
  235.0 0.0 copy-start.3
  235.0 0.0 copy-start.4
  235.0 0.0 copy-start.5
  235.1 2.6 copy.20
  237.6 0.0 copy-start
  237.7 0.5 fusion.17
  238.2 8.3 %collective-permute-start.3 = (bf16[64,2,1280]{2,1,0:T(2,128)(2,1)S(1)}, bf16[64,2,1280]{2,1,0:T(2,128)(2,1)S(1)}, u32[]{:S(2)}, u32[]{:S(2)}) collective-permute-start(bf16[64,2,1280]{2,1,0:T(2,128)(2,1)S(1)} %get-tuple-element.6), channel_id=1, source_target_pairs={{0,4},{4,8},{8,12},{12,16},{16,20},{20,24},{24,28},{1,5},{5,9},{9,... | collective-permute-start | bytes 983048 | tf_op jit(solution)/shard_map/ppermute | solution.py:37
  246.4 1.9 collective-permute-start.4
  248.4 2.9 collective-permute-done.3
  251.3 3.6 %collective-permute-done.4 = bf16[64,2,1280]{2,1,0:T(2,128)(2,1)S(1)} collective-permute-done((bf16[64,2,1280]{2,1,0:T(2,128)(2,1)S(1)}, bf16[64,2,1280]{2,1,0:T(2,128)(2,1)S(1)}, u32[]{:S(2)}, u32[]{:S(2)}) %collective-permute-start.4) | collective-permute-done | bytes 327712 | tf_op jit(solution)/shard_map/ppermute | solution.py:39
  254.8 0.5 pad_maximum_fusion.6
  255.3 0.1 collective-permute-start.5
  255.4 3.3 %collective-permute-start.6 = (bf16[64,20,2]{2,1,0:T(8,128)(2,1)S(1)}, bf16[64,20,2]{2,1,0:T(8,128)(2,1)S(1)}, u32[]{:S(2)}, u32[]{:S(2)}) collective-permute-start(bf16[64,20,2]{2,1,0:T(8,128)(2,1)S(1)} %get-tuple-element.5), channel_id=1, source_target_pairs={{1,0},{2,1},{3,2},{0,3},{5,4},{6,5},{7,6},{4,7},{9,8},{10,9},{11,1... | collective-permute-start | bytes 15368 | tf_op jit(solution)/shard_map/ppermute | solution.py:39
  258.7 0.0 copy-done.3
  258.7 0.0 copy-done.4
  258.7 0.0 copy-done.5
  258.7 0.1 fusion.10
  258.8 9.5 %collective-permute-done.5 = bf16[64,20,2]{2,1,0:T(8,128)(2,1)S(1)} collective-permute-done((bf16[64,20,2]{2,1,0:T(8,128)(2,1)S(1)}, bf16[64,20,2]{2,1,0:T(8,128)(2,1)S(1)}, u32[]{:S(2)}, u32[]{:S(2)}) %collective-permute-start.5) | collective-permute-done | bytes 5152 | tf_op jit(solution)/shard_map/ppermute | solution.py:37
  268.3 6.9 %collective-permute-done.6 = bf16[64,20,2]{2,1,0:T(8,128)(2,1)S(1)} collective-permute-done((bf16[64,20,2]{2,1,0:T(8,128)(2,1)S(1)}, bf16[64,20,2]{2,1,0:T(8,128)(2,1)S(1)}, u32[]{:S(2)}, u32[]{:S(2)}) %collective-permute-start.6) | collective-permute-done | bytes 5152 | tf_op jit(solution)/shard_map/ppermute | solution.py:39
  275.2 7.0 %maximum_maximum_fusion = (bf16[64,20,1282]{2,1,0:T(8,128)(2,1)S(1)}, bf16[64,20,1282]{2,1,0:T(8,128)(2,1)S(1)}) fusion(bf16[64,2,1280]{2,1,0:T(2,128)(2,1)S(1)} %collective-permute-done.4, bf16[64,16,1280]{2,1,0:T(8,128)(2,1)S(1)} %bitcast.123, bf16[64,2,1280]{2,1,0:T(2,128)(2,1)S(1)} %collective-permute-done.3, ...), kind=kLoop, calls=%fused_computation.15 | loop fusion | flops 26255360 | bytes 9850880 | tf_op jit(solution)/shard_map/concatenate | solution.py:35
  282.3 0.0 copy-done
  282.3 22.5 %add_convert_fusion = bf16[64,16,1280]{2,1,0:T(8,128)(2,1)} fusion(bf16[64,16,1280]{2,1,0:T(8,128)(2,1)S(1)} %bitcast.124, bf16[64,2,1280]{2,1,0:T(2,128)(2,1)S(1)} %collective-permute-done.4, bf16[64,20,1282]{2,1,0:T(8,128)(2,1)S(1)} %get-tuple-element.3, bf16[64,20,1282]{2,1,0:T(8,128)(2,1)S(1)} %get-tuple-element.2, ...), kind=kLoop, calls=%fused_computation.14 | loop fusion | flops 79953920 | bytes 38010880 | tf_op jit(solution)/shard_map/convert_element_type | solution.py:118
  (5 shorter events, 0.0 us)
Async XLA Ops:
  45.9 13.6 %copy-start.6 = (s32[1280]{0:T(1024)S(1)}, s32[1280]{0:T(1024)}, u32[]{:S(2)}) copy-start(s32[1280]{0:T(1024)} %param.8) | copy-start | bytes 15364
  54.9 19.1 %all-to-all-start = ((bf16[8,2,40960]{2,1,0:T(2,128)(2,1)}), bf16[8,2,40960]{2,1,0:T(2,128)(2,1)S(1)}, u32[]{:S(2)}, u32[]{:S(2)}) async-start(bf16[8,2,40960]{2,1,0:T(2,128)(2,1)} %reshape.307), calls=%async_computation | async-start | bytes 2621440 | tf_op jit(solution)/shard_map/all_to_all | solution.py:82
  97.2 41.0 %all-to-all-start.1 = ((bf16[320,1,4,16,2,16]{0,5,4,3,1,2:T(8,128)(2,1)}), bf16[320,1,4,16,2,16]{0,5,4,3,1,2:T(8,128)(2,1)S(1)}, u32[]{:S(2)}, u32[]{:S(2)}) async-start(bf16[320,1,4,16,2,16]{0,5,4,3,1,2:T(8,128)(2,1)} %bitcast.9), calls=%async_computation.1 | async-start | bytes 3145728 | tf_op jit(solution)/shard_map/all_to_all | solution.py:81
  140.7 30.9 %collective-permute-start = (bf16[1280,16,2,16]{0,3,2,1:T(8,128)(2,1)S(1)}, bf16[1280,16,2,16]{0,3,2,1:T(8,128)(2,1)S(1)}, u32[]{:S(2)}, u32[]{:S(2)}) collective-permute-start(bf16[1280,16,2,16]{0,3,2,1:T(8,128)(2,1)S(1)} %reshape.291), channel_id=1, source_target_pairs={{0,1},{1,2},{2,3},{3,0},{4,5},{5,6},{6,7},{7,4},{8,9},{9,10},{10,1... | collective-permute-start | bytes 3932168 | tf_op jit(solution)/shard_map/ppermute | solution.py:22
  141.0 30.6 %copy-start.1 = (bf16[1,1280,1280]{2,1,0:T(8,128)(2,1)S(1)}, bf16[1,1280,1280]{2,1,0:T(8,128)(2,1)}, u32[]{:S(2)}) copy-start(bf16[1,1280,1280]{2,1,0:T(8,128)(2,1)} %get-tuple-element.20) | copy-start | bytes 9830404
  141.0 30.6 %copy-start.2 = (bf16[1,1280,1280]{2,1,0:T(8,128)(2,1)S(1)}, bf16[1,1280,1280]{2,1,0:T(8,128)(2,1)}, u32[]{:S(2)}) copy-start(bf16[1,1280,1280]{2,1,0:T(8,128)(2,1)} %get-tuple-element.21) | copy-start | bytes 9830404
  171.6 29.7 %collective-permute-start.1 = (bf16[1280,16,2,16]{0,3,2,1:T(8,128)(2,1)S(1)}, bf16[1280,16,2,16]{0,3,2,1:T(8,128)(2,1)S(1)}, u32[]{:S(2)}, u32[]{:S(2)}) collective-permute-start(bf16[1280,16,2,16]{0,3,2,1:T(8,128)(2,1)S(1)} %collective-permute-done), channel_id=1, source_target_pairs={{0,1},{1,2},{2,3},{3,0},{4,5},{5,6},{6,7},{7,4},{8,9},{9,10},{10,1... | collective-permute-start | bytes 3932168 | tf_op jit(solution)/shard_map/ppermute | solution.py:22
  201.3 28.8 %collective-permute-start.2 = (bf16[1280,16,2,16]{0,3,2,1:T(8,128)(2,1)S(1)}, bf16[1280,16,2,16]{0,3,2,1:T(8,128)(2,1)S(1)}, u32[]{:S(2)}, u32[]{:S(2)}) collective-permute-start(bf16[1280,16,2,16]{0,3,2,1:T(8,128)(2,1)S(1)} %collective-permute-done.1), channel_id=1, source_target_pairs={{0,1},{1,2},{2,3},{3,0},{4,5},{5,6},{6,7},{7,4},{8,9},{9,10},{10,1... | collective-permute-start | bytes 3932168 | tf_op jit(solution)/shard_map/ppermute | solution.py:22
  235.0 23.6 %copy-start.3 = (f32[2,16,1280]{2,1,0:T(8,128)S(1)}, f32[2,16,1280]{2,1,0:T(8,128)}, u32[]{:S(2)}) copy-start(f32[2,16,1280]{2,1,0:T(8,128)} %param.11) | copy-start | bytes 491524
  235.0 23.6 %copy-start.4 = (s32[16,1280]{1,0:T(8,128)S(1)}, s32[16,1280]{1,0:T(8,128)}, u32[]{:S(2)}) copy-start(s32[16,1280]{1,0:T(8,128)} %param.9) | copy-start | bytes 245764
  235.0 23.6 %copy-start.5 = (s32[16,1280]{1,0:T(8,128)S(1)}, s32[16,1280]{1,0:T(8,128)}, u32[]{:S(2)}) copy-start(s32[16,1280]{1,0:T(8,128)} %param.10) | copy-start | bytes 245764
  237.6 44.6 %copy-start = (bf16[4,16,16,1280]{3,2,1,0:T(8,128)(2,1)}, bf16[4,16,16,1280]{3,2,1,0:T(8,128)(2,1)S(1)}, u32[]{:S(2)}) copy-start(bf16[4,16,16,1280]{3,2,1,0:T(8,128)(2,1)S(1)} %copy.20) | copy-start | bytes 7864324
  238.2 13.1 %collective-permute-start.3 = (bf16[64,2,1280]{2,1,0:T(2,128)(2,1)S(1)}, bf16[64,2,1280]{2,1,0:T(2,128)(2,1)S(1)}, u32[]{:S(2)}, u32[]{:S(2)}) collective-permute-start(bf16[64,2,1280]{2,1,0:T(2,128)(2,1)S(1)} %get-tuple-element.6), channel_id=1, source_target_pairs={{0,4},{4,8},{8,12},{12,16},{16,20},{20,24},{24,28},{1,5},{5,9},{9,... | collective-permute-start | bytes 983048 | tf_op jit(solution)/shard_map/ppermute | solution.py:37
  246.4 8.4 %collective-permute-start.4 = (bf16[64,2,1280]{2,1,0:T(2,128)(2,1)S(1)}, bf16[64,2,1280]{2,1,0:T(2,128)(2,1)S(1)}, u32[]{:S(2)}, u32[]{:S(2)}) collective-permute-start(bf16[64,2,1280]{2,1,0:T(2,128)(2,1)S(1)} %get-tuple-element.7), channel_id=1, source_target_pairs={{4,0},{8,4},{12,8},{16,12},{20,16},{24,20},{28,24},{5,1},{9,5},{13... | collective-permute-start | bytes 983048 | tf_op jit(solution)/shard_map/ppermute | solution.py:39
  255.3 13.0 %collective-permute-start.5 = (bf16[64,20,2]{2,1,0:T(8,128)(2,1)S(1)}, bf16[64,20,2]{2,1,0:T(8,128)(2,1)S(1)}, u32[]{:S(2)}, u32[]{:S(2)}) collective-permute-start(bf16[64,20,2]{2,1,0:T(8,128)(2,1)S(1)} %get-tuple-element.4), channel_id=1, source_target_pairs={{0,1},{1,2},{2,3},{3,0},{4,5},{5,6},{6,7},{7,4},{8,9},{9,10},{10,1... | collective-permute-start | bytes 15368 | tf_op jit(solution)/shard_map/ppermute | solution.py:37
  255.4 19.8 %collective-permute-start.6 = (bf16[64,20,2]{2,1,0:T(8,128)(2,1)S(1)}, bf16[64,20,2]{2,1,0:T(8,128)(2,1)S(1)}, u32[]{:S(2)}, u32[]{:S(2)}) collective-permute-start(bf16[64,20,2]{2,1,0:T(8,128)(2,1)S(1)} %get-tuple-element.5), channel_id=1, source_target_pairs={{1,0},{2,1},{3,2},{0,3},{5,4},{6,5},{7,6},{4,7},{9,8},{10,9},{11,1... | collective-permute-start | bytes 15368 | tf_op jit(solution)/shard_map/ppermute | solution.py:39
